TPU v7x, 32 devices: a whole 2x2x4 slice. The times are simulated.
32 devices in a mesh: groups: 2 (over y), sec: 4 (over x, core), plane: 4 (over z).
Axes of the slice: x: 2, y: 2, z: 4, core: 2. Of those that a mesh axis runs over, the one named last changes fastest.
Arguments:
- tokens: bfloat16 [16, 512, 1024], P(('groups', 'sec'), 'plane'), parts along dimension 0, may hold values from -8 to 8
- counts: int32 [16], P('groups'), parts along dimension 0, may hold values from 128 to 512, as said below
- region_ids: int32 [16, 512], P(('groups', 'sec'), 'plane'), parts along dimension 0, may hold values from 0 to 31
- norm_gains: float32 [2, 1024], replicated, may hold values from 0.1 to 1.9
- cross_qkv: bfloat16 [1024, 3072], P('plane'), may hold values from -2 to 2
- cross_out: bfloat16 [1024, 1024], P('plane'), may hold values from -0.1875 to 0.1875
- plane_qkv: bfloat16 [1024, 3072], P('plane'), may hold values from -2 to 2
- plane_out: bfloat16 [1024, 1024], P('plane'), may hold values from -0.1875 to 0.1875
Outputs:
- encoded: bfloat16 [16, 512, 1024], P(('groups', 'sec'), 'plane'), parts along dimension 0
- pooled: float32 [64, 1024], P(('groups', 'sec', 'plane')), parts along dimension 0
There are 2 independent parts, one for each index of `groups`. A program takes and returns all parts, laid end to end along the dimension named above; an argument that names none is the same for every part. Nothing has to cross between parts.
Inputs may be any that keep to these rules, and one draw needn't show every extreme that they name: `counts`: valid tissue tokens of each section; they are the first positions of the section.
All inputs are finite; a program needn't handle non-finite values.
Results may differ from a plain program's by a relative error of at most 0.009.
Values may be sent and summed in bfloat16 or wider, within the bound.
No kernel may reach another device: no remote copies, remote signals or barrier semaphores. Data moves between devices by JAX's collectives and lax.ppermute only.
A program may use at most 64 MiB of HBM per device.

v0:
```python
import math
import jax
import jax.numpy as jnp
from jax import lax
from jax.sharding import PartitionSpec as P

HEADS = 16
HEAD_DIM = 64
WINDOW = 128
negative_big = -1e30


def shifted_2(value, axis, by):
    peers = lax.axis_size(axis)
    pairs = [(i, i + by) for i in range(peers) if 0 <= i + by < peers]
    return lax.ppermute(value, axis, pairs)


def rms_norm(values, gain):
    wide = values.astype(jnp.float32)
    scaled = wide * lax.rsqrt(jnp.mean(wide * wide, axis=-1, keepdims=True) + 1e-06) * gain
    return scaled.astype(jnp.bfloat16)


def masked_softmax(scores, allowed):
    shifted = jnp.where(allowed, scores, negative_big)
    top = jnp.max(shifted, axis=-1, keepdims=True)
    expo = jnp.where(allowed, jnp.exp(shifted - top), 0.0)
    return (expo / jnp.sum(expo, axis=-1, keepdims=True)).astype(jnp.bfloat16)


def fold_product(inputs, weight_piece):
    return jnp.dot(inputs, weight_piece, preferred_element_type=jnp.float32)


def gather_pieces(shard):
    groups = lax.axis_size("groups")
    sections = lax.axis_size("sec")
    pair = 2 if sections % 2 == 0 else 1
    width = shard.shape[1] // (groups * pair)
    g = lax.axis_index("groups")
    k = lax.axis_index("sec") % pair
    own = g * pair + k
    mine = lax.dynamic_slice_in_dim(shard, own * width, width, axis=1)
    first = lax.all_gather(mine, "plane", axis=0, tiled=True)
    by_group = [(own, first)]
    for step in range(1, groups):
        moved = [(i, (i + step) % groups) for i in range(groups)]
        source = lax.rem(g - step + groups, groups)
        by_group.append((source * pair + k, lax.ppermute(first, "groups", moved)))
    held = list(by_group)
    if pair == 2:
        swap = [(i, i ^ 1) for i in range(sections)]
        for piece, block in by_group:
            held.append((piece - k + (1 - k), lax.ppermute(block, "sec", swap)))
    return (held, width)


def project(inputs, pieces):
    held, width = pieces
    out = jnp.zeros((inputs.shape[0], width * len(held)), jnp.float32)
    for piece, block in held:
        part = jnp.dot(inputs, block, preferred_element_type=jnp.float32)
        out = lax.dynamic_update_slice_in_dim(out, part, piece * width, axis=1)
    return out


def attend_items(pieces):
    packed_all, flags_all = pieces
    seq_len = packed_all.shape[2]
    block_len = 512
    score_scale = 1.0 / math.sqrt(HEAD_DIM)
    key_index = jnp.arange(seq_len, dtype=jnp.int32)

    def one_item(item_pair):
        packed, key_flag = item_pair
        key_rows = packed[:, HEAD_DIM : 2 * HEAD_DIM]
        value_rows = packed[:, 2 * HEAD_DIM :]
        key_alive = key_flag > 0.5
        query_blocks = packed[:, :HEAD_DIM].reshape(seq_len // block_len, block_len, HEAD_DIM)
        block_starts = jnp.arange(seq_len // block_len, dtype=jnp.int32) * block_len

        def one_block(block_pair):
            query_rows, offset = block_pair
            scores = (
                jnp.einsum("qd,kd->qk", query_rows, key_rows, preferred_element_type=jnp.float32)
                * score_scale
            )
            own_index = offset + jnp.arange(block_len, dtype=jnp.int32)
            allowed = key_alive[None, :] | (key_index[None, :] == own_index[:, None])
            attention = masked_softmax(scores, allowed)
            return jnp.dot(attention, value_rows, preferred_element_type=jnp.float32).astype(
                jnp.bfloat16
            )

        return lax.map(one_block, (query_blocks, block_starts)).reshape(seq_len, HEAD_DIM)

    return lax.map(one_item, (packed_all[0], flags_all[0]))[None]


def body(tokens, counts, region_ids, norm_gains, cross_qkv, cross_out, plane_qkv, plane_out):
    sec_block, tok_block, model_width = tokens.shape
    plane_count = lax.axis_size("plane")
    regions = 2 * lax.axis_size("sec") * plane_count
    positions = lax.axis_index("plane") * tok_block + jnp.arange(tok_block, dtype=jnp.int32)
    padded_counts = jnp.concatenate(
        [jnp.zeros((1,), jnp.int32), counts, jnp.zeros((1,), jnp.int32)]
    )
    near_counts = lax.dynamic_slice_in_dim(
        padded_counts, lax.axis_index("sec") * sec_block, sec_block + 2
    )
    near_valid = positions[None, :] < near_counts[:, None]
    own_valid = near_valid[1 : sec_block + 1]
    score_scale = 1.0 / math.sqrt(HEAD_DIM)
    cross_qkv_pieces = gather_pieces(cross_qkv)
    cross_out_pieces = gather_pieces(cross_out)
    plane_qkv_pieces = gather_pieces(plane_qkv)
    plane_out_pieces = gather_pieces(plane_out)
    normed = rms_norm(tokens, norm_gains[0])
    inputs = normed.reshape(-1, model_width)
    result = project(inputs, cross_qkv_pieces)
    projected = result.astype(jnp.bfloat16).reshape(sec_block, tok_block, 3 * model_width)
    own_kv = projected[:, :, model_width:]
    from_below = shifted_2(own_kv[sec_block - 1], "sec", 1)
    from_above = shifted_2(own_kv[0], "sec", -1)
    near_kv = jnp.concatenate([from_below[None], own_kv, from_above[None]], axis=0)
    queries = projected[:, :, :model_width]
    windows = tok_block // WINDOW
    query_win = queries.reshape(sec_block, windows, WINDOW, HEADS, HEAD_DIM)
    pair_win = near_kv.reshape(sec_block + 2, windows, WINDOW, 2, HEADS, HEAD_DIM)
    stacked = jnp.concatenate(
        [pair_win[0:sec_block], pair_win[1 : sec_block + 1], pair_win[2 : sec_block + 2]], axis=2
    )
    valid_win = near_valid.reshape(sec_block + 2, windows, WINDOW)
    valid_three = jnp.concatenate(
        [valid_win[0:sec_block], valid_win[1 : sec_block + 1], valid_win[2 : sec_block + 2]], axis=2
    )
    itself = jnp.arange(3 * WINDOW)[None, :] == jnp.arange(WINDOW)[:, None] + WINDOW
    scores = (
        jnp.einsum(
            "snqhd,snkhd->snhqk", query_win, stacked[:, :, :, 0], preferred_element_type=jnp.float32
        )
        * score_scale
    )
    allowed = valid_three[:, :, None, None, :] | itself[None, None, None]
    attention = masked_softmax(scores, allowed)
    context = jnp.einsum(
        "snhqk,snkhd->snqhd", attention, stacked[:, :, :, 1], preferred_element_type=jnp.float32
    )
    context = context.astype(jnp.bfloat16).reshape(-1, model_width)
    result = project(context, cross_out_pieces)
    after_cross = (tokens.reshape(-1, model_width).astype(jnp.float32) + result).astype(
        jnp.bfloat16
    )
    normed = rms_norm(after_cross, norm_gains[1])
    result = project(normed, plane_qkv_pieces)
    projected = result.astype(jnp.bfloat16).reshape(sec_block, tok_block, 3, HEADS, HEAD_DIM)
    per_device = sec_block * HEADS // plane_count
    heads_first = jnp.transpose(projected, (0, 3, 1, 2, 4)).reshape(
        plane_count, per_device, tok_block, 3 * HEAD_DIM
    )
    key_flags = jnp.broadcast_to(own_valid[:, None, :], (sec_block, HEADS, tok_block)).astype(
        jnp.bfloat16
    )
    key_flags = key_flags.reshape(plane_count, per_device, tok_block)
    attended = attend_items(
        (
            lax.all_to_all(heads_first, "plane", split_axis=0, concat_axis=2, tiled=True),
            lax.all_to_all(key_flags, "plane", split_axis=0, concat_axis=2, tiled=True),
        )
    )
    returned = lax.all_to_all(attended, "plane", split_axis=2, concat_axis=0, tiled=True)
    context = jnp.transpose(
        returned.reshape(sec_block, HEADS, tok_block, HEAD_DIM), (0, 2, 1, 3)
    ).reshape(-1, model_width)
    result = project(context, plane_out_pieces)
    encoded = (after_cross.astype(jnp.float32) + result).astype(jnp.bfloat16)
    labels = region_ids.reshape(-1)
    member = (jnp.arange(regions, dtype=jnp.int32)[:, None] == labels[None, :]) & own_valid.reshape(
        -1
    )[None, :]
    region_sum = jnp.dot(member.astype(jnp.bfloat16), encoded, preferred_element_type=jnp.float32)
    region_count = jnp.sum(member.astype(jnp.float32), axis=1)
    totals, counted = (
        lax.psum_scatter(region_sum, ("sec", "plane"), scatter_dimension=0, tiled=True),
        lax.psum_scatter(region_count, ("sec", "plane"), scatter_dimension=0, tiled=True),
    )
    pooled = totals / jnp.maximum(counted, 1.0)[:, None]
    return (encoded.reshape(sec_block, tok_block, model_width), pooled)


def solution(mesh):
    in_specs = (
        P(("groups", "sec"), "plane", None),
        P("groups"),
        P(("groups", "sec"), "plane"),
        P(),
        P("plane", None),
        P("plane", None),
        P("plane", None),
        P("plane", None),
    )
    out_specs = (P(("groups", "sec"), "plane", None), P(("groups", "sec", "plane"), None))
    return jax.shard_map(body, mesh=mesh, in_specs=in_specs, out_specs=out_specs, check_vma=False)
```

profile of v0, /device:TPU:8, one launch (start us, length us, event | category | flops | bytes accessed | tf_op | source)
XLA Modules:
  0.0 392.4 jit_solution(481135209715958584)
XLA Ops:
  9.4 1.8 constant_dynamic-slice_fusion.1
  11.2 35.6 %all-gather.3.cloned.1.call-done = bf16[1024,768]{1,0:T(8,128)(2,1)} async-done(((bf16[256,768]{1,0:T(8,128)(2,1)}), bf16[1024,768]{1,0:T(8,128)(2,1)}) %all-gather.3.cloned.1.call-update) | async-done | bytes 1572880 | tf_op jit(solution)/shard_map/all_gather | solution.py:45
  46.9 1.5 collective-permute-start
  49.2 18.7 %all_gather.13 = bf16[1024,256]{1,0:T(8,128)(2,1)} all-gather(bf16[256,256]{1,0:T(8,128)(2,1)S(1)} %constant_dynamic-slice_fusion.2), channel_id=1, replica_groups=mesh['groups'=2,'sec'=4,'plane'=4] {'plane'}, dimensions={0}, use_global_device_ids=true | all-gather | bytes 655360 | tf_op jit(solution)/shard_map/all_gather | solution.py:45
  69.2 15.3 %collective-permute-done = bf16[1024,768]{1,0:T(8,128)(2,1)} collective-permute-done((bf16[1024,768]{1,0:T(8,128)(2,1)}, bf16[1024,768]{1,0:T(8,128)(2,1)}, u32[]{:S(2)}, u32[]{:S(2)}) %collective-permute-start) | collective-permute-done | bytes 1572896 | tf_op jit(solution)/shard_map/ppermute | solution.py:50
  84.7 3.6 all-gather.5.cloned.1.call-done
  89.8 2.0 convolution_dynamic-update-slice_fusion.7
  91.8 2.0 convolution_dynamic-update-slice_fusion.6
  93.8 2.0 convolution_dynamic-update-slice_fusion.5
  95.8 2.0 convolution_dynamic-update-slice_fusion.4
  98.9 2.5 collective-permute-start.3
  101.4 1.5 collective-permute-start.4
  103.1 1.7 collective-permute-start.7
  107.7 20.3 %collective-permute-done.8 = bf16[1024,768]{1,0:T(8,128)(2,1)} collective-permute-done((bf16[1024,768]{1,0:T(8,128)(2,1)}, bf16[1024,768]{1,0:T(8,128)(2,1)}, u32[]{:S(2)}, u32[]{:S(2)}) %collective-permute-start.8) | collective-permute-done | bytes 1572896 | tf_op jit(solution)/shard_map/ppermute | solution.py:50
  128.5 2.7 pad_maximum_fusion.2
  131.3 2.4 copy.53
  135.0 2.0 pad_maximum_fusion
  138.0 3.2 fusion.56
  141.3 1.8 fusion.20
  151.6 2.0 convolution_dynamic-update-slice_fusion.2
  153.7 2.0 convolution_dynamic-update-slice_fusion.1
  155.8 2.0 convolution_dynamic-update-slice_fusion
  159.3 39.7 %all_to_all.45 = bf16[4,8,128,192]{2,3,1,0:T(8,128)(2,1)S(1)} all-to-all(bf16[4,8,128,192]{2,3,1,0:T(8,128)(2,1)S(1)} %bitcast.141), channel_id=1, replica_groups=mesh['groups'=2,'sec'=4,'plane'=4] {'plane'}, dimensions={0} | all-to-all | bytes 3145728 | tf_op jit(solution)/shard_map/all_to_all | solution.py:168
  199.7 5.0 %all-to-all-start = ((bf16[4,8,128]{2,1,0:T(8,128)(2,1)}), bf16[4,8,128]{2,1,0:T(8,128)(2,1)S(1)}, u32[]{:S(2)}, u32[]{:S(2)}) async-start(bf16[4,8,128]{2,1,0:T(8,128)(2,1)} %broadcast_in_dim.86), calls=%async_computation | async-start | bytes 16384 | tf_op jit(solution)/shard_map/all_to_all | solution.py:169
  204.7 2.6 copy.68
  207.3 1.6 all-to-all-done
  208.9 16.5 %while.11 = (s32[]{:T(128)}, bf16[8,512,64]{1,2,0:T(8,128)(2,1)S(1)}, bf16[8,512]{1,0:T(8,128)(2,1)S(1)}, bf16[8,512,192]{2,1,0:T(8,128)(2,1)}, s32[]{:T(128)}) while((s32[]{:T(128)}, bf16[8,512,64]{1,2,0:T(8,128)(2,1)S(1)}, bf16[8,512]{1,0:T(8,128)(2,1)S(1)}, bf16[8,512,192]{2,1,0:T(8,128)(2,1)}, s32[]{:T(128)}) %tuple.52), condition=%wide.region_7.8_spmd.clone, body=%wide.region_4.7_spmd.clone.sunk | while | flops 71336448 | bytes 3945545 | solution.py:98
  226.3 1.6 reshape.161
  227.8 4.8 %all-to-all-start.2 = ((bf16[4,2,32768]{2,1,0:T(2,128)(2,1)}), bf16[4,2,32768]{2,1,0:T(2,128)(2,1)S(1)}, u32[]{:S(2)}, u32[]{:S(2)}) async-start(bf16[4,2,32768]{2,1,0:T(2,128)(2,1)} %reshape.161), calls=%async_computation.2 | async-start | bytes 1048576 | tf_op jit(solution)/shard_map/all_to_all | solution.py:172
  233.5 21.6 %all_gather.15 = bf16[1024,256]{1,0:T(8,128)(2,1)S(1)} all-gather(bf16[256,256]{1,0:T(8,128)(2,1)S(1)} %constant_dynamic-slice_fusion), channel_id=1, replica_groups=mesh['groups'=2,'sec'=4,'plane'=4] {'plane'}, dimensions={0}, use_global_device_ids=true | all-gather | bytes 655360 | tf_op jit(solution)/shard_map/all_gather | solution.py:45
  258.0 30.8 %all-reduce.1 = f32[32]{0:T(128)S(1)} all-reduce(f32[32]{0:T(128)S(1)} %convert_reduce_fusion), channel_id=3, replica_groups=mesh['groups'=2,'sec'=4,'plane'=4] {'sec','plane'}, use_global_device_ids=true, to_apply=%region_10.11.clone | all-reduce | flops 32 | bytes 256
  295.0 89.5 %all-reduce.4.cloned.1.call-done = f32[32,1024]{1,0:T(8,128)} async-done(((f32[32,1024]{1,0:T(8,128)}), f32[32,1024]{1,0:T(8,128)}) %all-reduce.4.cloned.1.call-update) | async-done | bytes 131088
  (150 shorter events, 51.3 us)
Async XLA Ops:
  7.2 1.4 copy-start
  7.2 39.7 %all-gather.3.cloned.1.call-start = ((), (), s32[]{:S(2)}) async-start(), calls=%async_computation.3 | async-start | bytes 1966080 | tf_op jit(solution)/shard_map/all_gather | solution.py:45
  8.6 59.7 %copy-start.10 = (s32[8]{0:T(128)S(1)}, s32[8]{0:T(128)}, u32[]{:S(2)}) copy-start(s32[8]{0:T(128)} %param.11) | copy-start | bytes 100
  8.6 60.5 %copy-start.2 = (bf16[2,128,1024]{2,1,0:T(8,128)(2,1)S(1)}, bf16[2,128,1024]{2,1,0:T(8,128)(2,1)}, u32[]{:S(2)}) copy-start(bf16[2,128,1024]{2,1,0:T(8,128)(2,1)} %param.10) | copy-start | bytes 1572868
  9.4 75.1 %copy-start.7 = (f32[2,1024]{1,0:T(2,128)S(1)}, f32[2,1024]{1,0:T(2,128)}, u32[]{:S(2)}) copy-start(f32[2,1024]{1,0:T(2,128)} %param.13) | copy-start | bytes 24580
  9.4 78.9 %all-gather.5.cloned.1.call-start = ((), (), s32[]{:S(2)}) async-start(), calls=%async_computation.4 | async-start | bytes 1966080 | tf_op jit(solution)/shard_map/all_gather | solution.py:45
  46.9 37.6 %collective-permute-start = (bf16[1024,768]{1,0:T(8,128)(2,1)}, bf16[1024,768]{1,0:T(8,128)(2,1)}, u32[]{:S(2)}, u32[]{:S(2)}) collective-permute-start(bf16[1024,768]{1,0:T(8,128)(2,1)} %all-gather.3.cloned.1.call-done), channel_id=1, source_target_pairs={{0,16},{16,0},{1,17},{17,1},{2,18},{18,2},{3,19},{19,3},{4,20},{20... | collective-permute-start | bytes 4718600 | tf_op jit(solution)/shard_map/ppermute | solution.py:50
  67.9 35.1 %collective-permute-start.5 = (bf16[1024,256]{1,0:T(8,128)(2,1)}, bf16[1024,256]{1,0:T(8,128)(2,1)}, u32[]{:S(2)}, u32[]{:S(2)}) collective-permute-start(bf16[1024,256]{1,0:T(8,128)(2,1)} %all_gather.13), channel_id=1, source_target_pairs={{0,16},{16,0},{1,17},{17,1},{2,18},{18,2},{3,19},{19,3},{4,20},{20... | collective-permute-start | bytes 1572872 | tf_op jit(solution)/shard_map/ppermute | solution.py:50
  68.3 78.3 %collective-permute-start.6 = (bf16[1024,256]{1,0:T(8,128)(2,1)}, bf16[1024,256]{1,0:T(8,128)(2,1)}, u32[]{:S(2)}, u32[]{:S(2)}) collective-permute-start(bf16[1024,256]{1,0:T(8,128)(2,1)} %all_gather.13), channel_id=1, source_target_pairs={{0,4},{4,0},{8,12},{12,8},{1,5},{5,1},{9,13},{13,9},{2,6},{6,2},{1... | collective-permute-start | bytes 1572872 | tf_op jit(solution)/shard_map/ppermute | solution.py:55
  68.5 25.3 %collective-permute-start.1 = (bf16[1024,768]{1,0:T(8,128)(2,1)}, bf16[1024,768]{1,0:T(8,128)(2,1)}, u32[]{:S(2)}, u32[]{:S(2)}) collective-permute-start(bf16[1024,768]{1,0:T(8,128)(2,1)} %all-gather.3.cloned.1.call-done), channel_id=1, source_target_pairs={{0,4},{4,0},{8,12},{12,8},{1,5},{5,1},{9,13},{13,9},{2,6},{6,2},{1... | collective-permute-start | bytes 4718600 | tf_op jit(solution)/shard_map/ppermute | solution.py:55
  84.5 11.3 %collective-permute-start.2 = (bf16[1024,768]{1,0:T(8,128)(2,1)}, bf16[1024,768]{1,0:T(8,128)(2,1)}, u32[]{:S(2)}, u32[]{:S(2)}) collective-permute-start(bf16[1024,768]{1,0:T(8,128)(2,1)} %collective-permute-done), channel_id=1, source_target_pairs={{0,4},{4,0},{8,12},{12,8},{1,5},{5,1},{9,13},{13,9},{2,6},{6,2},{1... | collective-permute-start | bytes 4718600 | tf_op jit(solution)/shard_map/ppermute | solution.py:55
  88.3 39.8 %collective-permute-start.8 = (bf16[1024,768]{1,0:T(8,128)(2,1)}, bf16[1024,768]{1,0:T(8,128)(2,1)}, u32[]{:S(2)}, u32[]{:S(2)}) collective-permute-start(bf16[1024,768]{1,0:T(8,128)(2,1)} %all-gather.5.cloned.1.call-done), channel_id=1, source_target_pairs={{0,16},{16,0},{1,17},{17,1},{2,18},{18,2},{3,19},{19,3},{4,20},{20... | collective-permute-start | bytes 4718600 | tf_op jit(solution)/shard_map/ppermute | solution.py:50
  98.9 29.1 %collective-permute-start.3 = (bf16[128,2048]{1,0:T(8,128)(2,1)}, bf16[128,2048]{1,0:T(8,128)(2,1)}, u32[]{:S(2)}, u32[]{:S(2)}) collective-permute-start(bf16[128,2048]{1,0:T(8,128)(2,1)} %get-tuple-element.85), channel_id=1, source_target_pairs={{0,4},{4,8},{8,12},{1,5},{5,9},{9,13},{2,6},{6,10},{10,14},{3,7},{... | collective-permute-start | bytes 1572872 | tf_op jit(solution)/shard_map/ppermute | solution.py:16
  101.4 27.1 %collective-permute-start.4 = (bf16[128,2048]{1,0:T(8,128)(2,1)}, bf16[128,2048]{1,0:T(8,128)(2,1)}, u32[]{:S(2)}, u32[]{:S(2)}) collective-permute-start(bf16[128,2048]{1,0:T(8,128)(2,1)} %get-tuple-element.86), channel_id=1, source_target_pairs={{4,0},{8,4},{12,8},{5,1},{9,5},{13,9},{6,2},{10,6},{14,10},{7,3},{... | collective-permute-start | bytes 1572872 | tf_op jit(solution)/shard_map/ppermute | solution.py:16
  103.1 44.9 %collective-permute-start.7 = (bf16[1024,256]{1,0:T(8,128)(2,1)}, bf16[1024,256]{1,0:T(8,128)(2,1)}, u32[]{:S(2)}, u32[]{:S(2)}) collective-permute-start(bf16[1024,256]{1,0:T(8,128)(2,1)} %collective-permute-done.5), channel_id=1, source_target_pairs={{0,4},{4,0},{8,12},{12,8},{1,5},{5,1},{9,13},{13,9},{2,6},{6,2},{1... | collective-permute-start | bytes 1572872 | tf_op jit(solution)/shard_map/ppermute | solution.py:55
  128.0 25.7 %collective-permute-start.9 = (bf16[1024,768]{1,0:T(8,128)(2,1)}, bf16[1024,768]{1,0:T(8,128)(2,1)}, u32[]{:S(2)}, u32[]{:S(2)}) collective-permute-start(bf16[1024,768]{1,0:T(8,128)(2,1)} %all-gather.5.cloned.1.call-done), channel_id=1, source_target_pairs={{0,4},{4,0},{8,12},{12,8},{1,5},{5,1},{9,13},{13,9},{2,6},{6,2},{1... | collective-permute-start | bytes 4718600 | tf_op jit(solution)/shard_map/ppermute | solution.py:55
  128.0 27.7 %collective-permute-start.10 = (bf16[1024,768]{1,0:T(8,128)(2,1)}, bf16[1024,768]{1,0:T(8,128)(2,1)}, u32[]{:S(2)}, u32[]{:S(2)}) collective-permute-start(bf16[1024,768]{1,0:T(8,128)(2,1)} %collective-permute-done.8), channel_id=1, source_target_pairs={{0,4},{4,0},{8,12},{12,8},{1,5},{5,1},{9,13},{13,9},{2,6},{6,2},{1... | collective-permute-start | bytes 4718600 | tf_op jit(solution)/shard_map/ppermute | solution.py:55
  131.3 2.4 copy-start.3
  149.4 1.6 copy-start.9
  149.6 6.1 %copy-start.5 = (bf16[256,1024]{1,0:T(8,128)(2,1)}, bf16[256,1024]{1,0:T(8,128)(2,1)S(1)}, u32[]{:S(2)}) copy-start(bf16[256,1024]{1,0:T(8,128)(2,1)S(1)} %get-tuple-element.82) | copy-start | bytes 1572868
  199.7 9.2 %all-to-all-start = ((bf16[4,8,128]{2,1,0:T(8,128)(2,1)}), bf16[4,8,128]{2,1,0:T(8,128)(2,1)S(1)}, u32[]{:S(2)}, u32[]{:S(2)}) async-start(bf16[4,8,128]{2,1,0:T(8,128)(2,1)} %broadcast_in_dim.86), calls=%async_computation | async-start | bytes 16384 | tf_op jit(solution)/shard_map/all_to_all | solution.py:169
  226.2 30.4 %copy-start.8 = (s32[2,128]{1,0:T(2,128)S(1)}, s32[2,128]{1,0:T(2,128)}, u32[]{:S(2)}) copy-start(s32[2,128]{1,0:T(2,128)} %param.12) | copy-start | bytes 3076
  226.2 30.5 %copy-start.11 = (u32[32]{0:T(128)S(1)}, u32[32]{0:T(128)}, u32[]{:S(2)}) copy-start(u32[32]{0:T(128)} %constant.117) | copy-start | bytes 388
  227.8 61.1 %all-to-all-start.2 = ((bf16[4,2,32768]{2,1,0:T(2,128)(2,1)}), bf16[4,2,32768]{2,1,0:T(2,128)(2,1)S(1)}, u32[]{:S(2)}, u32[]{:S(2)}) async-start(bf16[4,2,32768]{2,1,0:T(2,128)(2,1)} %reshape.161), calls=%async_computation.2 | async-start | bytes 1048576 | tf_op jit(solution)/shard_map/all_to_all | solution.py:172
  232.6 151.8 %all-reduce.4.cloned.1.call-start = ((), (), s32[]{:S(2)}) async-start(), calls=%async_computation.5 | async-start | bytes 262144
  255.2 33.7 %collective-permute-start.11 = (bf16[1024,256]{1,0:T(8,128)(2,1)S(1)}, bf16[1024,256]{1,0:T(8,128)(2,1)S(1)}, u32[]{:S(2)}, u32[]{:S(2)}) collective-permute-start(bf16[1024,256]{1,0:T(8,128)(2,1)S(1)} %all_gather.15), channel_id=1, source_target_pairs={{0,16},{16,0},{1,17},{17,1},{2,18},{18,2},{3,19},{19,3},{4,20},{20... | collective-permute-start | bytes 1572872 | tf_op jit(solution)/shard_map/ppermute | solution.py:50
  256.6 35.4 %collective-permute-start.12 = (bf16[1024,256]{1,0:T(8,128)(2,1)S(1)}, bf16[1024,256]{1,0:T(8,128)(2,1)}, u32[]{:S(2)}, u32[]{:S(2)}) collective-permute-start(bf16[1024,256]{1,0:T(8,128)(2,1)S(1)} %all_gather.15), channel_id=1, source_target_pairs={{0,4},{4,0},{8,12},{12,8},{1,5},{5,1},{9,13},{13,9},{2,6},{6,2},{1... | collective-permute-start | bytes 1572872 | tf_op jit(solution)/shard_map/ppermute | solution.py:55
  288.9 4.7 %collective-permute-start.13 = (bf16[1024,256]{1,0:T(8,128)(2,1)S(1)}, bf16[1024,256]{1,0:T(8,128)(2,1)S(1)}, u32[]{:S(2)}, u32[]{:S(2)}) collective-permute-start(bf16[1024,256]{1,0:T(8,128)(2,1)S(1)} %collective-permute-done.11), channel_id=1, source_target_pairs={{0,4},{4,0},{8,12},{12,8},{1,5},{5,1},{9,13},{13,9},{2,6},{6,2},{1... | collective-permute-start | bytes 1572872 | tf_op jit(solution)/shard_map/ppermute | solution.py:55
  292.0 1.9 copy-start.6
  293.5 92.4 %copy-start.1 = (bf16[256,3072]{1,0:T(8,128)(2,1)S(1)}, bf16[256,3072]{1,0:T(8,128)(2,1)}, u32[]{:S(2)}) copy-start(bf16[256,3072]{1,0:T(8,128)(2,1)} %param.14) | copy-start | bytes 4718596
  294.0 91.9 %copy-start.4 = (bf16[256,1024]{1,0:T(8,128)(2,1)}, bf16[256,1024]{1,0:T(8,128)(2,1)S(1)}, u32[]{:S(2)}) copy-start(bf16[256,1024]{1,0:T(8,128)(2,1)S(1)} %fusion.24) | copy-start | bytes 1572868
Sparse Core Ops, SparseCore 0:
  9.6 37.2 all-gather.2
  49.0 39.2 all-gather.4
  295.0 89.3 all-reduce.3
where the time goes:
time: 394 us; the launch traced here: 392 us
  waiting for transfers between devices  166 us (42%)
  blocking collectives  111 us (28%)
  local copies, waits for them, and re-layouts  33.4 us (8%)
  matrix products  32.7 us (8%)
  starting transfers between devices  21.3 us (5%)
  between operations  15 us (4%)
  other arithmetic  12.9 us (3%)
    unnamed x4, waiting for transfers between devices  89.5 us
    all_gather x2, blocking collectives, gather_pieces(): first = lax.all_gather(mine, 'plane', axis=0, tiled=True)  40.4 us
    all_to_all x1, blocking collectives, body(): lax.all_to_all(heads_first, 'plane', split_axis=0, concat_axis=2, tiled=T...  39.7 us
    all_gather x2, waiting for transfers between devices, gather_pieces(): first = lax.all_gather(mine, 'plane', axis=0, tiled=True)  39.2 us
    ppermute x4, waiting for transfers between devices, gather_pieces(): by_group.append((source * pair + k, lax.ppermute(first, 'groups', moved)))  35.6 us
    unnamed x1, blocking collectives  30.8 us
    dot_general x16, matrix products, project(): part = jnp.dot(inputs, block, preferred_element_type=jnp.float32)  22.8 us
    unnamed x29, local copies, waits for them, and re-layouts  8.08 us
  transfers between devices with their start and end apart: 19, of which 6 were waited for; matrix products, arithmetic and copies ran while one was open for 13% of the time, Pallas kernels for 0%

commit v1 on v0

--- a/solution.py
+++ b/solution.py
@@ -42,7 +42,23 @@
     k = lax.axis_index("sec") % pair
     own = g * pair + k
     mine = lax.dynamic_slice_in_dim(shard, own * width, width, axis=1)
-    first = lax.all_gather(mine, "plane", axis=0, tiled=True)
+    placed = lax.psum(1, axis_name="plane")
+    local_now = lax.axis_index("plane")
+    latest, b_next, z = (placed, local_now, mine.shape[0])
+    views = [(rr, (rr + 1) % latest) for rr in range(latest)]
+    sides = [(rr, (rr - 1) % latest) for rr in range(latest)]
+    first = jnp.zeros((*mine.shape[:0], latest * z, *mine.shape[0 + 1 :]), mine.dtype)
+    first = lax.dynamic_update_slice_in_dim(first, mine, b_next * z, axis=0)
+    lower = val2 = mine
+    r_now = latest // 2
+    for tick in range(1, r_now + 1):
+        lower = lax.ppermute(lower, perm=views, axis_name="plane")
+        first = lax.dynamic_update_slice_in_dim(first, lower, (b_next - tick) % latest * z, axis=0)
+        if tick < latest - r_now:
+            val2 = lax.ppermute(val2, axis_name="plane", perm=sides)
+            first = lax.dynamic_update_slice_in_dim(
+                first, val2, (b_next + tick) % latest * z, axis=0
+            )
     by_group = [(own, first)]
     for step in range(1, groups):
         moved = [(i, (i + step) % groups) for i in range(groups)]

time: 394 us -> 379 us (0.962)
  blocking collectives: 111 us -> 30.8 us
  starting transfers between devices: 21.3 us -> 53.5 us
  waiting for transfers between devices: 166 us -> 188 us
  local copies, waits for them, and re-layouts: 33.4 us -> 44.4 us
    all_gather x2 -> x0, blocking collectives: 40.4 us -> none  [gather_pieces(): first = lax.all_gather(mine, 'plane', axis=0, tiled=True)]
    all_to_all x1 -> x0, blocking collectives: 39.7 us -> none  [body(): lax.all_to_all(heads_first, 'plane', split_axis=0, concat_axis=2, tiled=T...]
    all_gather x2 -> x0, waiting for transfers between devices: 39.2 us -> none  [gather_pieces(): first = lax.all_gather(mine, 'plane', axis=0, tiled=True)]
    all_to_all x0 -> x1, waiting for transfers between devices: none -> 32.6 us  [body(): lax.all_to_all(heads_first, 'plane', split_axis=0, concat_axis=2, tiled=T...]
    ppermute x0 -> x12, starting transfers between devices: none -> 19.8 us  [the longest x8 16.8 us: gather_pieces(): lower = lax.ppermute(lower, perm=views, axis_name='plane')]
    ppermute x0 -> x12, waiting for transfers between devices: none -> 16.5 us  [the longest x8 16.5 us: gather_pieces(): lower = lax.ppermute(lower, perm=views, axis_name='plane')]
    dynamic_update_slice x0 -> x16, local copies, waits for them, and re-layouts: none -> 14.4 us  [the longest x4 6.17 us: gather_pieces(): first = lax.dynamic_update_slice_in_dim(first, mine, b_next * z, axis=0)]
    ppermute x4, waiting for transfers between devices: 35.6 us -> 48.3 us  [gather_pieces(): by_group.append((source * pair + k, lax.ppermute(first, 'groups', moved)))]
  transfers between devices with their start and end apart: 19 -> 30, of which waited for: 6 -> 7; matrix products, arithmetic and copies ran while one was open for 13% -> 21% of each run, Pallas kernels for 0% -> 0%
where the time goes in v1:
time: 379 us; the launch traced here: 377 us
  waiting for transfers between devices  188 us (50%)
  starting transfers between devices  53.5 us (14%)
  local copies, waits for them, and re-layouts  44.4 us (12%)
  matrix products  31.2 us (8%)
  blocking collectives  30.8 us (8%)
  between operations  15.3 us (4%)
  other arithmetic  14.2 us (4%)
    unnamed x2, waiting for transfers between devices  90.1 us
    ppermute x4, waiting for transfers between devices, gather_pieces(): by_group.append((source * pair + k, lax.ppermute(first, 'groups', moved)))  48.3 us
    all_to_all x1, waiting for transfers between devices, body(): lax.all_to_all(heads_first, 'plane', split_axis=0, concat_axis=2, tiled=T...  32.6 us
    unnamed x1, blocking collectives  30.8 us
    dot_general x16, matrix products, project(): part = jnp.dot(inputs, block, preferred_element_type=jnp.float32)  21.3 us
    ppermute x8, starting transfers between devices, gather_pieces(): lower = lax.ppermute(lower, perm=views, axis_name='plane')  16.8 us
    ppermute x8, waiting for transfers between devices, gather_pieces(): lower = lax.ppermute(lower, perm=views, axis_name='plane')  16.5 us
    all_to_all x1, starting transfers between devices, body(): lax.all_to_all(key_flags, 'plane', split_axis=0, concat_axis=2, tiled=True)  8.02 us
  transfers between devices with their start and end apart: 30, of which 7 were waited for; matrix products, arithmetic and copies ran while one was open for 21% of the time, Pallas kernels for 0%

profile of v1, /device:TPU:8, one launch (start us, length us, event | category | flops | bytes accessed | tf_op | source)
XLA Modules:
  0.0 377.2 jit_solution(3114133574908750699)
XLA Ops:
  7.3 1.8 constant_dynamic-update-slice_fusion.15
  11.1 10.2 %collective-permute-done = bf16[256,768]{1,0:T(8,128)(2,1)S(1)} collective-permute-done((bf16[256,768]{1,0:T(8,128)(2,1)}, bf16[256,768]{1,0:T(8,128)(2,1)S(1)}, u32[]{:S(2)}, u32[]{:S(2)}) %collective-permute-start) | collective-permute-done | bytes 393248 | tf_op jit(solution)/shard_map/ppermute | solution.py:55
  21.3 7.8 %collective-permute-start.2 = (bf16[256,768]{1,0:T(8,128)(2,1)S(1)}, bf16[256,768]{1,0:T(8,128)(2,1)}, u32[]{:S(2)}, u32[]{:S(2)}) collective-permute-start(bf16[256,768]{1,0:T(8,128)(2,1)S(1)} %collective-permute-done), channel_id=1, source_target_pairs={{0,1},{1,2},{2,3},{3,0},{4,5},{5,6},{6,7},{7,4},{8,9},{9,10},{10,1... | collective-permute-start | bytes 1179656 | tf_op jit(solution)/shard_map/ppermute | solution.py:55
  31.5 1.7 collective-permute-start.8
  34.8 1.9 constant_dynamic-update-slice_fusion.7
  36.7 1.7 collective-permute-start.14
  44.3 2.2 collective-permute-start.15
  46.9 26.7 %collective-permute-done.3 = bf16[1024,768]{1,0:T(8,128)(2,1)} collective-permute-done((bf16[1024,768]{1,0:T(8,128)(2,1)S(1)}, bf16[1024,768]{1,0:T(8,128)(2,1)}, u32[]{:S(2)}, u32[]{:S(2)}) %collective-permute-start.3) | collective-permute-done | bytes 1572896 | tf_op jit(solution)/shard_map/ppermute | solution.py:66
  80.7 6.1 %collective-permute-done.16 = bf16[256,768]{1,0:T(8,128)(2,1)S(1)} collective-permute-done((bf16[256,768]{1,0:T(8,128)(2,1)S(1)}, bf16[256,768]{1,0:T(8,128)(2,1)S(1)}, u32[]{:S(2)}, u32[]{:S(2)}) %collective-permute-start.16) | collective-permute-done | bytes 393248 | tf_op jit(solution)/shard_map/ppermute | solution.py:55
  89.8 2.0 convolution_dynamic-update-slice_fusion.6
  91.8 2.0 convolution_dynamic-update-slice_fusion.5
  95.5 2.3 collective-permute-start.6
  99.4 1.9 collective-permute-start.12
  104.3 21.5 %collective-permute-done.17 = bf16[1024,768]{1,0:T(8,128)(2,1)} collective-permute-done((bf16[1024,768]{1,0:T(8,128)(2,1)}, bf16[1024,768]{1,0:T(8,128)(2,1)}, u32[]{:S(2)}, u32[]{:S(2)}) %collective-permute-start.17) | collective-permute-done | bytes 1572896 | tf_op jit(solution)/shard_map/ppermute | solution.py:66
  126.3 2.8 pad_maximum_fusion.2
  129.1 2.4 copy.53
  132.8 2.0 pad_maximum_fusion
  135.9 3.2 fusion.56
  139.1 1.8 fusion.20
  147.7 2.0 convolution_dynamic-update-slice_fusion.3
  149.7 2.0 convolution_dynamic-update-slice_fusion.2
  151.8 2.0 convolution_dynamic-update-slice_fusion.1
  153.8 2.0 convolution_dynamic-update-slice_fusion
  158.6 6.1 %all-to-all-start.1 = ((bf16[4,8,128,192]{2,3,1,0:T(8,128)(2,1)}), bf16[4,8,128,192]{2,3,1,0:T(8,128)(2,1)S(1)}, u32[]{:S(2)}, u32[]{:S(2)}) async-start(bf16[4,8,128,192]{2,3,1,0:T(8,128)(2,1)} %bitcast.26), calls=%async_computation.1 | async-start | bytes 3145728 | tf_op jit(solution)/shard_map/all_to_all | solution.py:184
  167.2 32.6 %all-to-all-done.1 = bf16[4,8,128,192]{2,3,1,0:T(8,128)(2,1)S(1)} async-done(((bf16[4,8,128,192]{2,3,1,0:T(8,128)(2,1)}), bf16[4,8,128,192]{2,3,1,0:T(8,128)(2,1)S(1)}, u32[]{:S(2)}, u32[]{:S(2)}) %all-to-all-start.1) | async-done | bytes 1572896 | tf_op jit(solution)/shard_map/all_to_all | solution.py:184
  200.5 8.0 %all-to-all-start = ((bf16[4,8,128]{2,1,0:T(8,128)(2,1)}), bf16[4,8,128]{2,1,0:T(8,128)(2,1)S(1)}, u32[]{:S(2)}, u32[]{:S(2)}) async-start(bf16[4,8,128]{2,1,0:T(8,128)(2,1)} %broadcast_in_dim.86), calls=%async_computation | async-start | bytes 16384 | tf_op jit(solution)/shard_map/all_to_all | solution.py:185
  208.6 1.9 collective-permute-start.22
  210.5 2.6 copy.68
  213.1 16.5 %while.11 = (s32[]{:T(128)}, bf16[8,512,64]{1,2,0:T(8,128)(2,1)S(1)}, bf16[8,512]{1,0:T(8,128)(2,1)S(1)}, bf16[8,512,192]{2,1,0:T(8,128)(2,1)}, s32[]{:T(128)}) while((s32[]{:T(128)}, bf16[8,512,64]{1,2,0:T(8,128)(2,1)S(1)}, bf16[8,512]{1,0:T(8,128)(2,1)S(1)}, bf16[8,512,192]{2,1,0:T(8,128)(2,1)}, s32[]{:T(128)}) %tuple.52), condition=%wide.region_7.8_spmd.clone, body=%wide.region_4.7_spmd.clone.sunk | while | flops 71336448 | bytes 3945545 | solution.py:114
  232.0 6.9 %all-to-all-start.2 = ((bf16[4,2,32768]{2,1,0:T(2,128)(2,1)}), bf16[4,2,32768]{2,1,0:T(2,128)(2,1)S(1)}, u32[]{:S(2)}, u32[]{:S(2)}) async-start(bf16[4,2,32768]{2,1,0:T(2,128)(2,1)} %reshape.161), calls=%async_computation.2 | async-start | bytes 1048576 | tf_op jit(solution)/shard_map/all_to_all | solution.py:188
  242.0 30.8 %all-reduce.1 = f32[32]{0:T(128)S(1)} all-reduce(f32[32]{0:T(128)S(1)} %convert_reduce_fusion), channel_id=3, replica_groups=mesh['groups'=2,'sec'=4,'plane'=4] {'sec','plane'}, use_global_device_ids=true, to_apply=%region_10.11.clone | all-reduce | flops 32 | bytes 256
  278.8 90.1 %all-reduce.4.cloned.1.call-done = f32[32,1024]{1,0:T(8,128)} async-done(((f32[32,1024]{1,0:T(8,128)}), f32[32,1024]{1,0:T(8,128)}) %all-reduce.4.cloned.1.call-update) | async-done | bytes 131088
  (179 shorter events, 72.5 us)
Async XLA Ops:
  9.1 12.2 %collective-permute-start = (bf16[256,768]{1,0:T(8,128)(2,1)}, bf16[256,768]{1,0:T(8,128)(2,1)S(1)}, u32[]{:S(2)}, u32[]{:S(2)}) collective-permute-start(bf16[256,768]{1,0:T(8,128)(2,1)} %get-tuple-element.84), channel_id=1, source_target_pairs={{0,1},{1,2},{2,3},{3,0},{4,5},{5,6},{6,7},{7,4},{8,9},{9,10},{10,1... | collective-permute-start | bytes 1179656 | tf_op jit(solution)/shard_map/ppermute | solution.py:55
  10.7 27.7 %collective-permute-start.1 = (bf16[256,768]{1,0:T(8,128)(2,1)}, bf16[256,768]{1,0:T(8,128)(2,1)}, u32[]{:S(2)}, u32[]{:S(2)}) collective-permute-start(bf16[256,768]{1,0:T(8,128)(2,1)} %get-tuple-element.84), channel_id=1, source_target_pairs={{0,3},{1,0},{2,1},{3,2},{4,7},{5,4},{6,5},{7,6},{8,11},{9,8},{10,9... | collective-permute-start | bytes 1179656 | tf_op jit(solution)/shard_map/ppermute | solution.py:58
  21.3 18.1 %collective-permute-start.2 = (bf16[256,768]{1,0:T(8,128)(2,1)S(1)}, bf16[256,768]{1,0:T(8,128)(2,1)}, u32[]{:S(2)}, u32[]{:S(2)}) collective-permute-start(bf16[256,768]{1,0:T(8,128)(2,1)S(1)} %collective-permute-done), channel_id=1, source_target_pairs={{0,1},{1,2},{2,3},{3,0},{4,5},{5,6},{6,7},{7,4},{8,9},{9,10},{10,1... | collective-permute-start | bytes 1179656 | tf_op jit(solution)/shard_map/ppermute | solution.py:55
  31.5 12.8 %collective-permute-start.8 = (bf16[256,256]{1,0:T(8,128)(2,1)S(1)}, bf16[256,256]{1,0:T(8,128)(2,1)}, u32[]{:S(2)}, u32[]{:S(2)}) collective-permute-start(bf16[256,256]{1,0:T(8,128)(2,1)S(1)} %get-tuple-element.86), channel_id=1, source_target_pairs={{0,1},{1,2},{2,3},{3,0},{4,5},{5,6},{6,7},{7,4},{8,9},{9,10},{10,1... | collective-permute-start | bytes 393224 | tf_op jit(solution)/shard_map/ppermute | solution.py:55
  33.2 13.3 %collective-permute-start.9 = (bf16[256,256]{1,0:T(8,128)(2,1)S(1)}, bf16[256,256]{1,0:T(8,128)(2,1)}, u32[]{:S(2)}, u32[]{:S(2)}) collective-permute-start(bf16[256,256]{1,0:T(8,128)(2,1)S(1)} %get-tuple-element.86), channel_id=1, source_target_pairs={{0,3},{1,0},{2,1},{3,2},{4,7},{5,4},{6,5},{7,6},{8,11},{9,8},{10,9... | collective-permute-start | bytes 393224 | tf_op jit(solution)/shard_map/ppermute | solution.py:58
  36.7 38.5 %collective-permute-start.14 = (bf16[256,768]{1,0:T(8,128)(2,1)S(1)}, bf16[256,768]{1,0:T(8,128)(2,1)S(1)}, u32[]{:S(2)}, u32[]{:S(2)}) collective-permute-start(bf16[256,768]{1,0:T(8,128)(2,1)S(1)} %get-tuple-element.88), channel_id=1, source_target_pairs={{0,1},{1,2},{2,3},{3,0},{4,5},{5,6},{6,7},{7,4},{8,9},{9,10},{10,1... | collective-permute-start | bytes 1179656 | tf_op jit(solution)/shard_map/ppermute | solution.py:55
  40.5 33.1 %collective-permute-start.3 = (bf16[1024,768]{1,0:T(8,128)(2,1)S(1)}, bf16[1024,768]{1,0:T(8,128)(2,1)}, u32[]{:S(2)}, u32[]{:S(2)}) collective-permute-start(bf16[1024,768]{1,0:T(8,128)(2,1)S(1)} %constant_dynamic-update-slice_fusion.12), channel_id=1, source_target_pairs={{0,16},{16,0},{1,17},{17,1},{2,18},{18,2},{3,19},{19,3},{4,20},{20... | collective-permute-start | bytes 4718600 | tf_op jit(solution)/shard_map/ppermute | solution.py:66
  42.7 49.1 %collective-permute-start.4 = (bf16[1024,768]{1,0:T(8,128)(2,1)S(1)}, bf16[1024,768]{1,0:T(8,128)(2,1)}, u32[]{:S(2)}, u32[]{:S(2)}) collective-permute-start(bf16[1024,768]{1,0:T(8,128)(2,1)S(1)} %constant_dynamic-update-slice_fusion.12), channel_id=1, source_target_pairs={{0,4},{4,0},{8,12},{12,8},{1,5},{5,1},{9,13},{13,9},{2,6},{6,2},{1... | collective-permute-start | bytes 4718600 | tf_op jit(solution)/shard_map/ppermute | solution.py:71
  44.3 35.6 %collective-permute-start.15 = (bf16[256,768]{1,0:T(8,128)(2,1)S(1)}, bf16[256,768]{1,0:T(8,128)(2,1)S(1)}, u32[]{:S(2)}, u32[]{:S(2)}) collective-permute-start(bf16[256,768]{1,0:T(8,128)(2,1)S(1)} %get-tuple-element.88), channel_id=1, source_target_pairs={{0,3},{1,0},{2,1},{3,2},{4,7},{5,4},{6,5},{7,6},{8,11},{9,8},{10,9... | collective-permute-start | bytes 1179656 | tf_op jit(solution)/shard_map/ppermute | solution.py:58
  46.5 30.5 %collective-permute-start.10 = (bf16[256,256]{1,0:T(8,128)(2,1)}, bf16[256,256]{1,0:T(8,128)(2,1)S(1)}, u32[]{:S(2)}, u32[]{:S(2)}) collective-permute-start(bf16[256,256]{1,0:T(8,128)(2,1)} %collective-permute-done.8), channel_id=1, source_target_pairs={{0,1},{1,2},{2,3},{3,0},{4,5},{5,6},{6,7},{7,4},{8,9},{9,10},{10,1... | collective-permute-start | bytes 393224 | tf_op jit(solution)/shard_map/ppermute | solution.py:55
  73.6 20.1 %collective-permute-start.5 = (bf16[1024,768]{1,0:T(8,128)(2,1)}, bf16[1024,768]{1,0:T(8,128)(2,1)S(1)}, u32[]{:S(2)}, u32[]{:S(2)}) collective-permute-start(bf16[1024,768]{1,0:T(8,128)(2,1)} %collective-permute-done.3), channel_id=1, source_target_pairs={{0,4},{4,0},{8,12},{12,8},{1,5},{5,1},{9,13},{13,9},{2,6},{6,2},{1... | collective-permute-start | bytes 4718600 | tf_op jit(solution)/shard_map/ppermute | solution.py:71
  75.2 11.5 %collective-permute-start.16 = (bf16[256,768]{1,0:T(8,128)(2,1)S(1)}, bf16[256,768]{1,0:T(8,128)(2,1)S(1)}, u32[]{:S(2)}, u32[]{:S(2)}) collective-permute-start(bf16[256,768]{1,0:T(8,128)(2,1)S(1)} %collective-permute-done.14), channel_id=1, source_target_pairs={{0,1},{1,2},{2,3},{3,0},{4,5},{5,6},{6,7},{7,4},{8,9},{9,10},{10,1... | collective-permute-start | bytes 1179656 | tf_op jit(solution)/shard_map/ppermute | solution.py:55
  77.6 23.7 %collective-permute-start.11 = (bf16[1024,256]{1,0:T(8,128)(2,1)}, bf16[1024,256]{1,0:T(8,128)(2,1)}, u32[]{:S(2)}, u32[]{:S(2)}) collective-permute-start(bf16[1024,256]{1,0:T(8,128)(2,1)} %constant_dynamic-update-slice_fusion.8), channel_id=1, source_target_pairs={{0,16},{16,0},{1,17},{17,1},{2,18},{18,2},{3,19},{19,3},{4,20},{20... | collective-permute-start | bytes 1572872 | tf_op jit(solution)/shard_map/ppermute | solution.py:66
  87.5 38.3 %collective-permute-start.17 = (bf16[1024,768]{1,0:T(8,128)(2,1)}, bf16[1024,768]{1,0:T(8,128)(2,1)}, u32[]{:S(2)}, u32[]{:S(2)}) collective-permute-start(bf16[1024,768]{1,0:T(8,128)(2,1)} %constant_dynamic-update-slice_fusion.4), channel_id=1, source_target_pairs={{0,16},{16,0},{1,17},{17,1},{2,18},{18,2},{3,19},{19,3},{4,20},{20... | collective-permute-start | bytes 4718600 | tf_op jit(solution)/shard_map/ppermute | solution.py:66
  95.5 30.4 %collective-permute-start.6 = (bf16[128,2048]{1,0:T(8,128)(2,1)}, bf16[128,2048]{1,0:T(8,128)(2,1)}, u32[]{:S(2)}, u32[]{:S(2)}) collective-permute-start(bf16[128,2048]{1,0:T(8,128)(2,1)} %get-tuple-element.93), channel_id=1, source_target_pairs={{0,4},{4,8},{8,12},{1,5},{5,9},{9,13},{2,6},{6,10},{10,14},{3,7},{... | collective-permute-start | bytes 1572872 | tf_op jit(solution)/shard_map/ppermute | solution.py:16
  97.8 28.5 %collective-permute-start.7 = (bf16[128,2048]{1,0:T(8,128)(2,1)}, bf16[128,2048]{1,0:T(8,128)(2,1)}, u32[]{:S(2)}, u32[]{:S(2)}) collective-permute-start(bf16[128,2048]{1,0:T(8,128)(2,1)} %get-tuple-element.94), channel_id=1, source_target_pairs={{4,0},{8,4},{12,8},{5,1},{9,5},{13,9},{6,2},{10,6},{14,10},{7,3},{... | collective-permute-start | bytes 1572872 | tf_op jit(solution)/shard_map/ppermute | solution.py:16
  99.4 45.0 %collective-permute-start.12 = (bf16[1024,256]{1,0:T(8,128)(2,1)}, bf16[1024,256]{1,0:T(8,128)(2,1)}, u32[]{:S(2)}, u32[]{:S(2)}) collective-permute-start(bf16[1024,256]{1,0:T(8,128)(2,1)} %constant_dynamic-update-slice_fusion.8), channel_id=1, source_target_pairs={{0,4},{4,0},{8,12},{12,8},{1,5},{5,1},{9,13},{13,9},{2,6},{6,2},{1... | collective-permute-start | bytes 1572872 | tf_op jit(solution)/shard_map/ppermute | solution.py:71
  101.3 44.5 %collective-permute-start.13 = (bf16[1024,256]{1,0:T(8,128)(2,1)}, bf16[1024,256]{1,0:T(8,128)(2,1)}, u32[]{:S(2)}, u32[]{:S(2)}) collective-permute-start(bf16[1024,256]{1,0:T(8,128)(2,1)} %collective-permute-done.11), channel_id=1, source_target_pairs={{0,4},{4,0},{8,12},{12,8},{1,5},{5,1},{9,13},{13,9},{2,6},{6,2},{1... | collective-permute-start | bytes 1572872 | tf_op jit(solution)/shard_map/ppermute | solution.py:71
  125.8 26.0 %collective-permute-start.18 = (bf16[1024,768]{1,0:T(8,128)(2,1)}, bf16[1024,768]{1,0:T(8,128)(2,1)}, u32[]{:S(2)}, u32[]{:S(2)}) collective-permute-start(bf16[1024,768]{1,0:T(8,128)(2,1)} %constant_dynamic-update-slice_fusion.4), channel_id=1, source_target_pairs={{0,4},{4,0},{8,12},{12,8},{1,5},{5,1},{9,13},{13,9},{2,6},{6,2},{1... | collective-permute-start | bytes 4718600 | tf_op jit(solution)/shard_map/ppermute | solution.py:71
  125.8 28.0 %collective-permute-start.19 = (bf16[1024,768]{1,0:T(8,128)(2,1)}, bf16[1024,768]{1,0:T(8,128)(2,1)}, u32[]{:S(2)}, u32[]{:S(2)}) collective-permute-start(bf16[1024,768]{1,0:T(8,128)(2,1)} %collective-permute-done.17), channel_id=1, source_target_pairs={{0,4},{4,0},{8,12},{12,8},{1,5},{5,1},{9,13},{13,9},{2,6},{6,2},{1... | collective-permute-start | bytes 4718600 | tf_op jit(solution)/shard_map/ppermute | solution.py:71
  158.6 41.3 %copy-start.7 = (bf16[2,128]{1,0:T(2,128)(2,1)S(1)}, bf16[2,128]{1,0:T(2,128)(2,1)}, u32[]{:S(2)}) copy-start(bf16[2,128]{1,0:T(2,128)(2,1)} %get-tuple-element.100) | copy-start | bytes 1540
  158.6 41.3 %all-to-all-start.1 = ((bf16[4,8,128,192]{2,3,1,0:T(8,128)(2,1)}), bf16[4,8,128,192]{2,3,1,0:T(8,128)(2,1)S(1)}, u32[]{:S(2)}, u32[]{:S(2)}) async-start(bf16[4,8,128,192]{2,3,1,0:T(8,128)(2,1)} %bitcast.26), calls=%async_computation.1 | async-start | bytes 3145728 | tf_op jit(solution)/shard_map/all_to_all | solution.py:184
  165.7 42.9 %collective-permute-start.20 = (bf16[256,256]{1,0:T(8,128)(2,1)S(1)}, bf16[256,256]{1,0:T(8,128)(2,1)S(1)}, u32[]{:S(2)}, u32[]{:S(2)}) collective-permute-start(bf16[256,256]{1,0:T(8,128)(2,1)S(1)} %get-tuple-element.90), channel_id=1, source_target_pairs={{0,1},{1,2},{2,3},{3,0},{4,5},{5,6},{6,7},{7,4},{8,9},{9,10},{10,1... | collective-permute-start | bytes 393224 | tf_op jit(solution)/shard_map/ppermute | solution.py:55
  200.5 12.6 %all-to-all-start = ((bf16[4,8,128]{2,1,0:T(8,128)(2,1)}), bf16[4,8,128]{2,1,0:T(8,128)(2,1)S(1)}, u32[]{:S(2)}, u32[]{:S(2)}) async-start(bf16[4,8,128]{2,1,0:T(8,128)(2,1)} %broadcast_in_dim.86), calls=%async_computation | async-start | bytes 16384 | tf_op jit(solution)/shard_map/all_to_all | solution.py:185
  208.5 30.4 %collective-permute-start.21 = (bf16[256,256]{1,0:T(8,128)(2,1)S(1)}, bf16[256,256]{1,0:T(8,128)(2,1)S(1)}, u32[]{:S(2)}, u32[]{:S(2)}) collective-permute-start(bf16[256,256]{1,0:T(8,128)(2,1)S(1)} %get-tuple-element.90), channel_id=1, source_target_pairs={{0,3},{1,0},{2,1},{3,2},{4,7},{5,4},{6,5},{7,6},{8,11},{9,8},{10,9... | collective-permute-start | bytes 393224 | tf_op jit(solution)/shard_map/ppermute | solution.py:58
  208.6 30.3 %collective-permute-start.22 = (bf16[256,256]{1,0:T(8,128)(2,1)S(1)}, bf16[256,256]{1,0:T(8,128)(2,1)S(1)}, u32[]{:S(2)}, u32[]{:S(2)}) collective-permute-start(bf16[256,256]{1,0:T(8,128)(2,1)S(1)} %collective-permute-done.20), channel_id=1, source_target_pairs={{0,1},{1,2},{2,3},{3,0},{4,5},{5,6},{6,7},{7,4},{8,9},{9,10},{10,1... | collective-permute-start | bytes 393224 | tf_op jit(solution)/shard_map/ppermute | solution.py:55
  232.0 40.8 %all-to-all-start.2 = ((bf16[4,2,32768]{2,1,0:T(2,128)(2,1)}), bf16[4,2,32768]{2,1,0:T(2,128)(2,1)S(1)}, u32[]{:S(2)}, u32[]{:S(2)}) async-start(bf16[4,2,32768]{2,1,0:T(2,128)(2,1)} %reshape.161), calls=%async_computation.2 | async-start | bytes 1048576 | tf_op jit(solution)/shard_map/all_to_all | solution.py:188
  238.9 130.1 %all-reduce.4.cloned.1.call-start = ((), (), s32[]{:S(2)}) async-start(), calls=%async_computation.3 | async-start | bytes 262144
  239.0 33.8 %collective-permute-start.23 = (bf16[1024,256]{1,0:T(8,128)(2,1)S(1)}, bf16[1024,256]{1,0:T(8,128)(2,1)S(1)}, u32[]{:S(2)}, u32[]{:S(2)}) collective-permute-start(bf16[1024,256]{1,0:T(8,128)(2,1)S(1)} %constant_dynamic-update-slice_fusion), channel_id=1, source_target_pairs={{0,16},{16,0},{1,17},{17,1},{2,18},{18,2},{3,19},{19,3},{4,20},{20... | collective-permute-start | bytes 1572872 | tf_op jit(solution)/shard_map/ppermute | solution.py:66
  240.6 35.3 %collective-permute-start.24 = (bf16[1024,256]{1,0:T(8,128)(2,1)S(1)}, bf16[1024,256]{1,0:T(8,128)(2,1)S(1)}, u32[]{:S(2)}, u32[]{:S(2)}) collective-permute-start(bf16[1024,256]{1,0:T(8,128)(2,1)S(1)} %constant_dynamic-update-slice_fusion), channel_id=1, source_target_pairs={{0,4},{4,0},{8,12},{12,8},{1,5},{5,1},{9,13},{13,9},{2,6},{6,2},{1... | collective-permute-start | bytes 1572872 | tf_op jit(solution)/shard_map/ppermute | solution.py:71
  272.8 3.5 collective-permute-start.25
  277.9 92.5 %copy-start.2 = (bf16[256,1024]{1,0:T(8,128)(2,1)}, bf16[256,1024]{1,0:T(8,128)(2,1)S(1)}, u32[]{:S(2)}) copy-start(bf16[256,1024]{1,0:T(8,128)(2,1)S(1)} %fusion.24) | copy-start | bytes 1572868
  (8 other events, 51.6 us)
Sparse Core Ops, SparseCore 0:
  278.9 90.0 all-reduce.3
